TPU v7x, 256 devices: a whole 4x4x8 slice. The times are simulated.
256 devices in a mesh: dp: 8 (over x, core), seq: 32 (over y, z).
Axes of the slice: x: 4, y: 4, z: 8, core: 2. Of those that a mesh axis runs over, the one named last changes fastest.
Arguments:
- activations: bfloat16 [8, 4096, 2048], P('dp', 'seq'), may hold values from -16 to 16
- w_query: bfloat16 [2048, 2048], P('seq')
- w_key: bfloat16 [2048, 256], P('seq')
- w_value: bfloat16 [2048, 256], P('seq'), may hold values from -0.125 to 0.125
- key_blocks: int32 [32, 32, 7], replicated, may hold values from 0 to 31, as said below
- random_count: int32 [32], replicated, may hold values from 1 to 3, 64 in all
- grad_out: bfloat16 [8, 4096, 2048], P('dp', 'seq'), may hold values from -6 to 6
Outputs:
- attn_out: bfloat16 [8, 4096, 2048], P('dp', 'seq')
- grad_x: bfloat16 [8, 4096, 2048], P('dp', 'seq')
- grad_wq: bfloat16 [2048, 2048], P('seq')
- grad_wk: bfloat16 [2048, 256], P('seq')
- grad_wv: bfloat16 [2048, 256], P('seq')
Inputs may be any that keep to these rules, and one draw needn't show every extreme that they name: `key_blocks`: row b of head h: columns 0 to 2 are b - 1, b and b + 1 modulo 32; column 3 is one block of the head, the same in all its rows; columns 4 to 6 are three blocks that differ from each other and from the row's first four entries. Head h uses the first random_count[h] of its three random key blocks; the counts sum to 64.
All inputs are finite; a program needn't handle non-finite values.
Results may differ from a plain program's by a relative error of at most 0.025.
The roundings to bfloat16 on the way count: a program that leaves them out, or rounds other values in their place, can miss the bound.
Values may be sent and summed in bfloat16 or wider, within the bound.
No kernel may reach another device: no remote copies, remote signals or barrier semaphores. Data moves between devices by JAX's collectives and lax.ppermute only.
A program may use at most 128 MiB of HBM per device.

v0:
```python
import math
import jax
import jax.numpy as jnp
from jax import lax
from jax.sharding import PartitionSpec as P

HD = 64
GROUP = 8
masked_score = -1e30
query_group = 4


def head_pass(queries, key_rows, value_rows, grad_head, blocks, extra_count):
    seq_len, head_width = queries.shape
    block_count, slot_count = blocks.shape
    block_len = seq_len // block_count
    score_scale = head_width ** (-0.5)
    key_tiles = key_rows.reshape(block_count, block_len, head_width)
    value_tiles = value_rows.reshape(block_count, block_len, head_width)
    usable = jnp.repeat(jnp.arange(slot_count) < 4 + extra_count, block_len)
    rounds = block_count // query_group
    query_steps = queries.reshape(rounds, query_group, block_len, head_width)
    grad_steps = grad_head.reshape(rounds, query_group, block_len, head_width)
    block_steps = blocks.reshape(rounds, query_group, slot_count)

    def one_step(running, inputs):
        q_part, g_part, chosen = inputs
        k_part = key_tiles[chosen].reshape(query_group, slot_count * block_len, head_width)
        v_part = value_tiles[chosen].reshape(query_group, slot_count * block_len, head_width)
        scores = (
            jnp.einsum("gqe,gke->gqk", q_part, k_part, preferred_element_type=jnp.float32)
            * score_scale
        )
        scores = jnp.where(usable, scores, masked_score)
        highest = jnp.max(scores, axis=-1, keepdims=True)
        exponent = jnp.exp(scores - highest)
        shares = exponent / jnp.sum(exponent, axis=-1, keepdims=True)
        shares_low = shares.astype(jnp.bfloat16)
        attended = jnp.einsum(
            "gqk,gke->gqe", shares_low, v_part, preferred_element_type=jnp.float32
        ).astype(jnp.bfloat16)
        grad_shares = jnp.einsum("gqe,gke->gqk", g_part, v_part, preferred_element_type=jnp.float32)
        weighted = jnp.sum(grad_shares * shares, axis=-1, keepdims=True)
        grad_scores = (shares * (grad_shares - weighted)).astype(jnp.bfloat16)
        grad_query = (
            jnp.einsum("gqk,gke->gqe", grad_scores, k_part, preferred_element_type=jnp.float32)
            * score_scale
        ).astype(jnp.bfloat16)
        grad_keys = (
            jnp.einsum("gqk,gqe->gke", grad_scores, q_part, preferred_element_type=jnp.float32)
            * score_scale
        )
        grad_values = jnp.einsum(
            "gqk,gqe->gke", shares_low, g_part, preferred_element_type=jnp.float32
        )
        pieces = jnp.concatenate([grad_keys, grad_values], axis=-1).reshape(
            query_group * slot_count, block_len, 2 * head_width
        )
        running = running.at[chosen.reshape(-1)].add(pieces)
        return (running, (attended, grad_query))

    initial = jnp.zeros((block_count, block_len, 2 * head_width), jnp.float32)
    summed, (attended, grad_query) = lax.scan(
        one_step, initial, (query_steps, grad_steps, block_steps)
    )
    return (
        attended.reshape(seq_len, head_width),
        grad_query.reshape(seq_len, head_width),
        summed.reshape(seq_len, 2 * head_width),
    )


def per_device(activations, w_query, w_key, w_value, key_blocks, random_count, grad_out):
    seq_devices = lax.axis_size("seq")
    dp_devices = lax.axis_size("dp")
    position = lax.axis_index("seq")
    dp_index = lax.axis_index("dp")
    tokens = activations[0]
    grad_rows = grad_out[0]
    tok_count = tokens.shape[0]
    heads = w_query.shape[1] // HD
    kv_heads = w_key.shape[1] // HD
    query_cols = heads * HD
    kv_cols = kv_heads * HD
    all_cols = query_cols + 2 * kv_cols
    w_local = jnp.concatenate([w_query, w_key, w_value], axis=1)
    w_full = lax.all_gather(w_local, "seq", axis=0, tiled=True)
    projected = jnp.dot(tokens, w_full, preferred_element_type=jnp.float32).astype(jnp.bfloat16)
    queries = projected[:, :query_cols]
    key_proj = projected[:, query_cols : query_cols + kv_cols]
    value_proj = projected[:, query_cols + kv_cols :]
    query_pieces = queries.reshape(tok_count, heads, HD).transpose(1, 0, 2)
    grad_pieces = grad_rows.reshape(tok_count, heads, HD).transpose(1, 0, 2)
    paired = jnp.concatenate(
        [key_proj.reshape(tok_count, kv_heads, HD), value_proj.reshape(tok_count, kv_heads, HD)],
        axis=2,
    )
    kv_pieces = jnp.repeat(paired.transpose(1, 0, 2), GROUP, axis=0)
    sent = jnp.concatenate([query_pieces, grad_pieces, kv_pieces], axis=2)
    landed = lax.all_to_all(sent, "seq", split_axis=0, concat_axis=1, tiled=True)[0]
    head_q = landed[:, :HD]
    head_grad = landed[:, HD : 2 * HD]
    head_k = landed[:, 2 * HD : 3 * HD]
    head_v = landed[:, 3 * HD :]
    blocks_mine = lax.dynamic_index_in_dim(key_blocks, position, 0, keepdims=False)
    count_mine = lax.dynamic_index_in_dim(random_count, position, 0, keepdims=False)
    attended, grad_query, grad_kv = head_pass(
        head_q, head_k, head_v, head_grad, blocks_mine, count_mine
    )
    back_sent = jnp.concatenate(
        [
            attended.reshape(seq_devices, tok_count, HD),
            grad_query.reshape(seq_devices, tok_count, HD),
            grad_kv.astype(jnp.bfloat16).reshape(seq_devices, tok_count, 2 * HD),
        ],
        axis=2,
    )
    back = lax.all_to_all(back_sent, "seq", split_axis=0, concat_axis=0, tiled=True)
    back_out = back[:, :, :HD]
    back_query = back[:, :, HD : 2 * HD]
    back_kv = back[:, :, 2 * HD :]
    out_rows = back_out.transpose(1, 0, 2).reshape(tok_count, heads * HD)
    grad_q_rows = back_query.transpose(1, 0, 2).reshape(tok_count, heads * HD)
    kv_sum = jnp.sum(
        back_kv.reshape(kv_heads, GROUP, tok_count, 2 * HD), axis=1, dtype=jnp.float32
    ).astype(jnp.bfloat16)
    grad_k_rows = kv_sum[:, :, :HD].transpose(1, 0, 2).reshape(tok_count, kv_heads * HD)
    grad_v_rows = kv_sum[:, :, HD:].transpose(1, 0, 2).reshape(tok_count, kv_heads * HD)
    combined = jnp.concatenate([grad_q_rows, grad_k_rows, grad_v_rows], axis=1)
    contract = (((1,), (1,)), ((), ()))
    grad_x_rows = lax.dot_general(
        combined, w_full, contract, preferred_element_type=jnp.float32
    ).astype(jnp.bfloat16)
    factor = 1.0 / math.sqrt(tok_count * seq_devices * dp_devices)
    over_tokens = (((0,), (0,)), ((), ()))
    term = (
        lax.dot_general(tokens, combined, over_tokens, preferred_element_type=jnp.float32) * factor
    ).astype(jnp.bfloat16)
    half = all_cols // 2
    core = dp_index % 2
    pairs = [(i, i ^ 1) for i in range(dp_devices)]
    keep = lax.dynamic_slice_in_dim(term, core * half, half, axis=1)
    give = lax.dynamic_slice_in_dim(term, (1 - core) * half, half, axis=1)
    got = lax.ppermute(give, "dp", pairs)
    chip_sum = (keep.astype(jnp.float32) + got.astype(jnp.float32)).astype(jnp.bfloat16)
    part = lax.psum_scatter(chip_sum, "seq", scatter_dimension=0, tiled=True)
    step = 2
    while step < dp_devices:
        mates = [(i, i ^ step) for i in range(dp_devices)]
        other = lax.ppermute(part, "dp", mates)
        part = (part.astype(jnp.float32) + other.astype(jnp.float32)).astype(jnp.bfloat16)
        step *= 2
    other_half = lax.ppermute(part, "dp", pairs)
    first = jnp.where(core == 0, part, other_half)
    second = jnp.where(core == 0, other_half, part)
    grad_all = jnp.concatenate([first, second], axis=1)
    grad_wq = grad_all[:, :query_cols]
    grad_wk = grad_all[:, query_cols : query_cols + kv_cols]
    grad_wv = grad_all[:, query_cols + kv_cols :]
    return (out_rows[None], grad_x_rows[None], grad_wq, grad_wk, grad_wv)


def solution(mesh):
    placed = (
        P("dp", "seq", None),
        P("seq", None),
        P("seq", None),
        P("seq", None),
        P(),
        P(),
        P("dp", "seq", None),
    )
    return jax.shard_map(
        per_device,
        mesh=mesh,
        in_specs=placed,
        out_specs=(
            P("dp", "seq", None),
            P("dp", "seq", None),
            P("seq", None),
            P("seq", None),
            P("seq", None),
        ),
        check_vma=False,
    )
```

profile of v0, /device:TPU:7, one launch (start us, length us, event | category | flops | bytes accessed | tf_op | source)
XLA Modules:
  0.0 728.5 jit_solution(3099953773682184216)
XLA Ops:
  10.4 112.5 %all-gather.2.cloned.1.call-done = bf16[2048,2560]{1,0:T(8,128)(2,1)} async-done(((bf16[64,2560]{1,0:T(8,128)(2,1)}), bf16[2048,2560]{1,0:T(8,128)(2,1)}) %all-gather.2.cloned.1.call-update) | async-done | bytes 10485776 | tf_op jit(solution)/shard_map/all_gather | solution.py:87
  122.8 6.9 fusion.43
  131.6 5.4 all-to-all-start
  139.2 46.5 %all-to-all-done = bf16[32,128,256]{1,2,0:T(8,128)(2,1)S(1)} async-done(((bf16[32,128,256]{1,2,0:T(8,128)(2,1)}), bf16[32,128,256]{1,2,0:T(8,128)(2,1)S(1)}, u32[]{:S(2)}, u32[]{:S(2)}) %all-to-all-start) | async-done | bytes 2097184 | tf_op jit(solution)/shard_map/all_to_all | solution.py:100
  199.0 167.2 %while.15 = (s32[]{:T(128)}, f32[32,128,128]{2,1,0:T(8,128)}, bf16[8,4,128,64]{2,3,1,0:T(8,128)(2,1)}, bf16[8,4,128,64]{2,3,1,0:T(8,128)(2,1)}, s32[8,4,7]{2,1,0...) while((s32[]{:T(128)}, f32[32,128,128]{2,1,0:T(8,128)}, ...), condition=%wide.region_5.6_spmd.clone, body=%wide.region_0.5_spmd.clone.sunk | while | flops 360449568 | bytes 45045204 | solution.py:63
  213.1 6.9 scatter_fusion
  234.0 6.9 scatter_fusion
  254.9 6.8 scatter_fusion
  275.8 6.8 scatter_fusion
  296.7 6.9 scatter_fusion
  317.6 6.8 scatter_fusion
  338.5 6.8 scatter_fusion
  359.4 6.8 scatter_fusion
  369.7 7.2 all-to-all-start.1
  377.1 49.0 %all-to-all-done.1 = bf16[32,128,256]{1,2,0:T(8,128)(2,1)S(1)} async-done(((bf16[32,128,256]{1,2,0:T(8,128)(2,1)}), bf16[32,128,256]{1,2,0:T(8,128)(2,1)S(1)}, u32[]{:S(2)}, u32[]{:S(2)}) %all-to-all-start.1) | async-done | bytes 2097184 | tf_op jit(solution)/shard_map/all_to_all | solution.py:118
  427.2 5.1 multiply_convert_fusion.1
  439.7 8.6 %collective-permute-done = bf16[2048,1280]{0,1:T(8,128)(2,1)} collective-permute-done((bf16[2048,1280]{0,1:T(8,128)(2,1)}, bf16[2048,1280]{0,1:T(8,128)(2,1)}, u32[]{:S(2)}, u32[]{:S(2)}) %collective-permute-start) | collective-permute-done | bytes 5242912 | tf_op jit(solution)/shard_map/ppermute | solution.py:144
  448.3 9.4 %fusion.42 = bf16[2048,1280]{0,1:T(8,128)(2,1)} fusion(bf16[2048,1280]{0,1:T(8,128)(2,1)} %collective-permute-done, bf16[2560,2048]{1,0:T(8,128)(2,1)} %copy-done.1, s32[]{:T(128)S(6)} %select_n.59), kind=kLoop, calls=%fused_computation.54 | loop fusion | flops 10485760 | bytes 15728644 | tf_op jit(solution)/shard_map/convert_element_type | solution.py:145
  457.7 7.9 %copy.86 = bf16[2048,1280]{1,0:T(8,128)(2,1)} copy(bf16[2048,1280]{0,1:T(8,128)(2,1)} %fusion.42) | data formatting | bytes 10485760
  465.7 218.4 %reduce-scatter.4.cloned.1.call-done = bf16[64,1280]{1,0:T(8,128)(2,1)} async-done(((bf16[2048,1280]{1,0:T(8,128)(2,1)}), bf16[64,1280]{1,0:T(8,128)(2,1)}) %reduce-scatter.4.cloned.1.call-update) | async-done | bytes 163856
  685.5 5.7 collective-permute-done.1
  692.1 8.1 %collective-permute-done.2 = bf16[64,1280]{0,1:T(8,128)(2,1)S(1)} collective-permute-done((bf16[64,1280]{0,1:T(8,128)(2,1)S(1)}, bf16[64,1280]{0,1:T(8,128)(2,1)S(1)}, u32[]{:S(2)}, u32[]{:S(2)}) %collective-permute-start.2) | collective-permute-done | bytes 163872 | tf_op jit(solution)/shard_map/ppermute | solution.py:150
  700.4 9.5 %collective-permute-start.3 = (bf16[64,1280]{0,1:T(8,128)(2,1)S(1)}, bf16[64,1280]{0,1:T(8,128)(2,1)S(1)}, u32[]{:S(2)}, u32[]{:S(2)}) collective-permute-start(bf16[64,1280]{0,1:T(8,128)(2,1)S(1)} %add_convert_fusion), channel_id=1, source_target_pairs={{0,32},{32,0},{64,96},{96,64},{128,160},{160,128},{192,224},{224,1... | collective-permute-start | bytes 491528 | tf_op jit(solution)/shard_map/ppermute | solution.py:153
  709.9 8.3 %fusion.44 = bf16[1,128,2048]{2,1,0:T(8,128)(2,1)} fusion(bf16[2048,2560]{1,0:T(8,128)(2,1)} %all-gather.2.cloned.1.call-done, bf16[128,256]{0,1:T(8,128)(2,1)S(1)} %bitcast.151, bf16[128,256]{0,1:T(8,128)(2,1)S(1)} %bitcast.149, bf16[128,2048]{0,1:T(8,128)(2,1)S(1)} %bitcast.141), kind=kOutput, calls=%fused_computation.59 | convolution fusion | flops 1344405504 | bytes 11665408 | tf_op jit(solution)/shard_map/dot_general | solution.py:131
  (270 shorter events, 149.7 us)
Async XLA Ops:
  7.2 115.7 %copy-start = (bf16[1,128,2048]{2,1,0:T(8,128)(2,1)S(1)}, bf16[1,128,2048]{2,1,0:T(8,128)(2,1)}, u32[]{:S(2)}) copy-start(bf16[1,128,2048]{2,1,0:T(8,128)(2,1)} %param.9) | copy-start | bytes 1572868
  7.2 115.7 %all-gather.2.cloned.1.call-start = ((), (), s32[]{:S(2)}) async-start(), calls=%async_computation.3 | async-start | bytes 10813440 | tf_op jit(solution)/shard_map/all_gather | solution.py:87
  131.6 54.1 %all-to-all-start = ((bf16[32,128,256]{1,2,0:T(8,128)(2,1)}), bf16[32,128,256]{1,2,0:T(8,128)(2,1)S(1)}, u32[]{:S(2)}, u32[]{:S(2)}) async-start(bf16[32,128,256]{1,2,0:T(8,128)(2,1)} %pad_maximum_fusion.1), calls=%async_computation | async-start | bytes 4194304 | tf_op jit(solution)/shard_map/all_to_all | solution.py:100
  213.1 6.9 copy-start.3
  213.1 6.9 copy-start.5
  234.0 6.9 copy-start.3
  234.0 6.9 copy-start.5
  254.9 6.8 copy-start.5
  275.8 6.8 copy-start.3
  275.8 6.8 copy-start.5
  296.7 6.9 copy-start.3
  296.7 6.9 copy-start.5
  317.6 6.8 copy-start.5
  338.5 6.8 copy-start.3
  338.5 6.8 copy-start.5
  359.4 6.8 copy-start.3
  359.4 6.8 copy-start.5
  369.7 56.4 %all-to-all-start.1 = ((bf16[32,128,256]{1,2,0:T(8,128)(2,1)}), bf16[32,128,256]{1,2,0:T(8,128)(2,1)S(1)}, u32[]{:S(2)}, u32[]{:S(2)}) async-start(bf16[32,128,256]{1,2,0:T(8,128)(2,1)} %pad_maximum_fusion.2), calls=%async_computation.1 | async-start | bytes 4194304 | tf_op jit(solution)/shard_map/all_to_all | solution.py:118
  376.9 307.2 %reduce-scatter.4.cloned.1.call-start = ((), (), s32[]{:S(2)}) async-start(), calls=%async_computation.4 | async-start | bytes 5406720
  437.8 10.6 %collective-permute-start = (bf16[2048,1280]{0,1:T(8,128)(2,1)}, bf16[2048,1280]{0,1:T(8,128)(2,1)}, u32[]{:S(2)}, u32[]{:S(2)}) collective-permute-start(bf16[2048,1280]{0,1:T(8,128)(2,1)} %dynamic-slice_bitcast_fusion), channel_id=1, source_target_pairs={{0,32},{32,0},{64,96},{96,64},{128,160},{160,128},{192,224},{224,1... | collective-permute-start | bytes 15728648 | tf_op jit(solution)/shard_map/ppermute | solution.py:144
  685.2 6.0 collective-permute-start.1
  691.3 9.0 %collective-permute-start.2 = (bf16[64,1280]{0,1:T(8,128)(2,1)S(1)}, bf16[64,1280]{0,1:T(8,128)(2,1)S(1)}, u32[]{:S(2)}, u32[]{:S(2)}) collective-permute-start(bf16[64,1280]{0,1:T(8,128)(2,1)S(1)} %add_convert_fusion.1), channel_id=1, source_target_pairs={{0,128},{32,160},{64,192},{96,224},{128,0},{160,32},{192,64},{224,... | collective-permute-start | bytes 491528 | tf_op jit(solution)/shard_map/ppermute | solution.py:150
  700.4 17.8 %copy-start.7 = (bf16[32,128,64]{1,2,0:T(8,128)(2,1)S(1)}, bf16[32,128,64]{1,2,0:T(8,128)(2,1)}, u32[]{:S(2)}) copy-start(bf16[32,128,64]{1,2,0:T(8,128)(2,1)} %get-tuple-element.162) | copy-start | bytes 1572868
  700.4 18.8 %collective-permute-start.3 = (bf16[64,1280]{0,1:T(8,128)(2,1)S(1)}, bf16[64,1280]{0,1:T(8,128)(2,1)S(1)}, u32[]{:S(2)}, u32[]{:S(2)}) collective-permute-start(bf16[64,1280]{0,1:T(8,128)(2,1)S(1)} %add_convert_fusion), channel_id=1, source_target_pairs={{0,32},{32,0},{64,96},{96,64},{128,160},{160,128},{192,224},{224,1... | collective-permute-start | bytes 491528 | tf_op jit(solution)/shard_map/ppermute | solution.py:153
  (30 other events, 75.9 us)
Sparse Core Ops, SparseCore 0:
  11.2 111.6 all-gather.1
  465.8 218.2 reduce-scatter.3
where the time goes:
time: 731 us; the launch traced here: 729 us
  waiting for transfers between devices  449 us (61%)
  matrix products  93.4 us (13%)
  other arithmetic  73.4 us (10%)
  local copies, waits for them, and re-layouts  72 us (10%)
  starting transfers between devices  25.4 us (3%)
  between operations  14.9 us (2%)
    unnamed x3, waiting for transfers between devices  218 us
    all_gather x1, waiting for transfers between devices, per_device(): w_full = lax.all_gather(w_local, 'seq', axis=0, tiled=True)  112 us
    scatter-add x8, other arithmetic, one_step(): running = running.at[chosen.reshape(-1)].add(pieces)  54.7 us
    all_to_all x1, waiting for transfers between devices, per_device(): lax.all_to_all(back_sent, 'seq', split_axis=0, concat_axis=0, tiled=True)  49 us
    all_to_all x1, waiting for transfers between devices, per_device(): lax.all_to_all(sent, 'seq', split_axis=0, concat_axis=1, tiled=True)[0]  46.5 us
    unnamed x21, local copies, waits for them, and re-layouts  20.6 us
    dot_general x8, matrix products, one_step(): jnp.einsum('gqk,gke->gqe', shares_low, v_part, preferred_element_type=jnp...  19.1 us
  transfers between devices with their start and end apart: 8, of which 7 were waited for; matrix products, arithmetic and copies ran while one was open for 2% of the time, Pallas kernels for 0%

commit v1 on v0

--- a/solution.py
+++ b/solution.py
@@ -1,3 +1,4 @@
+import functools
 import math
 import jax
 import jax.numpy as jnp
@@ -8,6 +9,17 @@
 GROUP = 8
 masked_score = -1e30
 query_group = 4
+
+
+def test_numbers(v0, dim_at, along_dim):
+    reply = jnp.concatenate(
+        lax.all_to_all(jnp.stack(jnp.split(v0, lax.psum(1, "seq"), axis=dim_at)), "seq", 0, 0),
+        axis=along_dim,
+    )
+    return reply
+
+
+point_classes = functools.partial(test_numbers, dim_at=0, along_dim=1)
 
 
 def head_pass(queries, key_rows, value_rows, grad_head, blocks, extra_count):
@@ -97,7 +109,7 @@
     )
     kv_pieces = jnp.repeat(paired.transpose(1, 0, 2), GROUP, axis=0)
     sent = jnp.concatenate([query_pieces, grad_pieces, kv_pieces], axis=2)
-    landed = lax.all_to_all(sent, "seq", split_axis=0, concat_axis=1, tiled=True)[0]
+    landed = point_classes(sent)[0]
     head_q = landed[:, :HD]
     head_grad = landed[:, HD : 2 * HD]
     head_k = landed[:, 2 * HD : 3 * HD]

time: 731 us -> 736 us (level)
  local copies, waits for them, and re-layouts: 72 us -> 105 us
  matrix products: 93.4 us -> 65.7 us
    unnamed x21 -> x52, local copies, waits for them, and re-layouts: 20.6 us -> 36.6 us
    dynamic_slice x0 -> x8, local copies, waits for them, and re-layouts: none -> 7.78 us  [head_pass(): lax.scan(one_step, initial, (query_steps, grad_steps, block_steps))]
    dot_general x8, matrix products: 10.3 us -> 2.97 us  [one_step(): jnp.einsum('gqk,gqe->gke', shares_low, g_part, preferred_element_type=jnp...]
where the time goes in v1:
time: 736 us; the launch traced here: 734 us
  waiting for transfers between devices  446 us (61%)
  local copies, waits for them, and re-layouts  105 us (14%)
  other arithmetic  74 us (10%)
  matrix products  65.7 us (9%)
  starting transfers between devices  27.2 us (4%)
  between operations  15 us (2%)
    unnamed x3, waiting for transfers between devices  218 us
    all_gather x1, waiting for transfers between devices, per_device(): w_full = lax.all_gather(w_local, 'seq', axis=0, tiled=True)  112 us
    scatter-add x8, other arithmetic, one_step(): running = running.at[chosen.reshape(-1)].add(pieces)  55.9 us
    all_to_all x1, waiting for transfers between devices, per_device(): lax.all_to_all(back_sent, 'seq', split_axis=0, concat_axis=0, tiled=True)  48.6 us
    all_to_all x1, waiting for transfers between devices, test_numbers(): lax.all_to_all(jnp.stack(jnp.split(v0, lax.psum(1, 'seq'), axis=dim_at)),...  46.3 us
    unnamed x52, local copies, waits for them, and re-layouts  36.6 us
    dot_general x8, matrix products, one_step(): jnp.einsum('gqk,gke->gqe', shares_low, v_part, preferred_element_type=jnp...  19.1 us
  transfers between devices with their start and end apart: 8, of which 7 were waited for; matrix products, arithmetic and copies ran while one was open for 2% of the time, Pallas kernels for 0%

profile of v1, /device:TPU:7, one launch (start us, length us, event | category | flops | bytes accessed | tf_op | source)
XLA Modules:
  0.0 734.0 jit_solution(5973791993855364121)
XLA Ops:
  10.9 112.0 %all-gather.2.cloned.1.call-done = bf16[2048,2560]{1,0:T(8,128)(2,1)} async-done(((bf16[64,2560]{1,0:T(8,128)(2,1)}), bf16[2048,2560]{1,0:T(8,128)(2,1)}) %all-gather.2.cloned.1.call-update) | async-done | bytes 10485776 | tf_op jit(solution)/shard_map/all_gather | solution.py:99
  122.8 6.9 fusion.23
  151.7 5.6 all-to-all-start
  159.5 46.3 %all-to-all-done = bf16[32,1,128,256]{3,2,1,0:T(8,128)(2,1)S(1)} async-done(((bf16[32,1,128,256]{3,2,1,0:T(8,128)(2,1)}), bf16[32,1,128,256]{3,2,1,0:T(8,128)(2,1)S(1)}, u32[]{:S(2)}, u32[]{:S(2)}) %all-to-all-start) | async-done | bytes 2097184 | tf_op jit(solution)/shard_map/all_to_all | solution.py:16
  216.8 155.2 %while.15 = (s32[]{:T(128)}, f32[32,128,128]{2,1,0:T(8,128)}, bf16[8,4,128,64]{2,3,1,0:T(8,128)(2,1)}, bf16[8,4,128,64]{2,3,1,0:T(8,128)(2,1)}, s32[8,4,7]{2,1,0...) while((s32[]{:T(128)}, f32[32,128,128]{2,1,0:T(8,128)}, ...), condition=%wide.region_5.6_spmd.clone, body=%wide.region_0.5_spmd.clone.sunk | while | flops 360449568 | bytes 49501696 | solution.py:75
  229.1 7.0 scatter_fusion
  248.5 7.0 scatter_fusion
  268.0 7.0 scatter_fusion
  287.4 7.0 scatter_fusion
  306.8 7.0 scatter_fusion
  326.2 6.9 scatter_fusion
  345.5 7.0 scatter_fusion
  365.0 7.0 scatter_fusion
  375.5 7.1 all-to-all-start.1
  382.6 48.6 %all-to-all-done.1 = bf16[32,128,256]{1,2,0:T(8,128)(2,1)S(1)} async-done(((bf16[32,128,256]{1,2,0:T(8,128)(2,1)}), bf16[32,128,256]{1,2,0:T(8,128)(2,1)S(1)}, u32[]{:S(2)}, u32[]{:S(2)}) %all-to-all-start.1) | async-done | bytes 2097184 | tf_op jit(solution)/shard_map/all_to_all | solution.py:130
  432.3 5.1 multiply_convert_fusion.1
  445.4 8.6 %collective-permute-done = bf16[2048,1280]{0,1:T(8,128)(2,1)} collective-permute-done((bf16[2048,1280]{0,1:T(8,128)(2,1)}, bf16[2048,1280]{0,1:T(8,128)(2,1)}, u32[]{:S(2)}, u32[]{:S(2)}) %collective-permute-start) | collective-permute-done | bytes 5242912 | tf_op jit(solution)/shard_map/ppermute | solution.py:156
  454.0 9.5 %fusion.22 = bf16[2048,1280]{0,1:T(8,128)(2,1)} fusion(bf16[2048,1280]{0,1:T(8,128)(2,1)} %collective-permute-done, bf16[2560,2048]{1,0:T(8,128)(2,1)} %copy-done.1, s32[]{:T(128)S(6)} %select_n.59), kind=kLoop, calls=%fused_computation.43 | loop fusion | flops 10485760 | bytes 15728644 | tf_op jit(solution)/shard_map/convert_element_type | solution.py:157
  463.5 7.8 %copy.146 = bf16[2048,1280]{1,0:T(8,128)(2,1)} copy(bf16[2048,1280]{0,1:T(8,128)(2,1)} %fusion.22) | data formatting | bytes 10485760
  471.3 218.0 %reduce-scatter.4.cloned.1.call-done = bf16[64,1280]{1,0:T(8,128)(2,1)} async-done(((bf16[2048,1280]{1,0:T(8,128)(2,1)}), bf16[64,1280]{1,0:T(8,128)(2,1)}) %reduce-scatter.4.cloned.1.call-update) | async-done | bytes 163856
  691.6 5.0 collective-permute-done.1
  698.3 7.7 %collective-permute-done.2 = bf16[64,1280]{0,1:T(8,128)(2,1)S(1)} collective-permute-done((bf16[64,1280]{0,1:T(8,128)(2,1)S(1)}, bf16[64,1280]{0,1:T(8,128)(2,1)S(1)}, u32[]{:S(2)}, u32[]{:S(2)}) %collective-permute-start.2) | collective-permute-done | bytes 163872 | tf_op jit(solution)/shard_map/ppermute | solution.py:162
  706.2 9.2 %collective-permute-start.3 = (bf16[64,1280]{0,1:T(8,128)(2,1)S(1)}, bf16[64,1280]{0,1:T(8,128)(2,1)S(1)}, u32[]{:S(2)}, u32[]{:S(2)}) collective-permute-start(bf16[64,1280]{0,1:T(8,128)(2,1)S(1)} %add_convert_fusion), channel_id=1, source_target_pairs={{0,32},{32,0},{64,96},{96,64},{128,160},{160,128},{192,224},{224,1... | collective-permute-start | bytes 491528 | tf_op jit(solution)/shard_map/ppermute | solution.py:165
  715.4 8.3 %fusion.24 = bf16[1,128,2048]{2,1,0:T(8,128)(2,1)} fusion(bf16[2048,2560]{1,0:T(8,128)(2,1)} %all-gather.2.cloned.1.call-done, bf16[128,256]{0,1:T(8,128)(2,1)S(1)} %bitcast.276, bf16[128,256]{0,1:T(8,128)(2,1)S(1)} %bitcast.274, bf16[128,2048]{0,1:T(8,128)(2,1)S(1)} %bitcast.265), kind=kOutput, calls=%fused_computation.48 | convolution fusion | flops 1344405504 | bytes 11665408 | tf_op jit(solution)/shard_map/dot_general | solution.py:143
  (346 shorter events, 156.5 us)
Async XLA Ops:
  7.2 115.7 %copy-start = (bf16[1,128,2048]{2,1,0:T(8,128)(2,1)S(1)}, bf16[1,128,2048]{2,1,0:T(8,128)(2,1)}, u32[]{:S(2)}) copy-start(bf16[1,128,2048]{2,1,0:T(8,128)(2,1)} %param.9) | copy-start | bytes 1572868
  7.2 115.7 %all-gather.2.cloned.1.call-start = ((), (), s32[]{:S(2)}) async-start(), calls=%async_computation.3 | async-start | bytes 10813440 | tf_op jit(solution)/shard_map/all_gather | solution.py:99
  151.7 54.1 %all-to-all-start = ((bf16[32,1,128,256]{3,2,1,0:T(8,128)(2,1)}), bf16[32,1,128,256]{3,2,1,0:T(8,128)(2,1)S(1)}, u32[]{:S(2)}, u32[]{:S(2)}) async-start(bf16[32,1,128,256]{3,2,1,0:T(8,128)(2,1)} %constant_dynamic-update-slice_fusion), calls=%async_computation | async-start | bytes 4194304 | tf_op jit(solution)/shard_map/all_to_all | solution.py:16
  248.5 7.0 copy-start.3
  248.5 7.0 copy-start.5
  248.5 7.0 copy-start.10
  287.4 7.0 copy-start.3
  287.4 7.0 copy-start.5
  287.4 7.0 copy-start.10
  306.8 7.0 copy-start.5
  306.8 7.0 copy-start.10
  345.5 7.0 copy-start.3
  345.5 7.0 copy-start.5
  345.5 7.0 copy-start.10
  365.0 7.0 copy-start.3
  365.0 7.0 copy-start.5
  365.0 7.0 copy-start.10
  375.5 55.8 %all-to-all-start.1 = ((bf16[32,128,256]{1,2,0:T(8,128)(2,1)}), bf16[32,128,256]{1,2,0:T(8,128)(2,1)S(1)}, u32[]{:S(2)}, u32[]{:S(2)}) async-start(bf16[32,128,256]{1,2,0:T(8,128)(2,1)} %pad_maximum_fusion.2), calls=%async_computation.1 | async-start | bytes 4194304 | tf_op jit(solution)/shard_map/all_to_all | solution.py:130
  382.6 306.8 %reduce-scatter.4.cloned.1.call-start = ((), (), s32[]{:S(2)}) async-start(), calls=%async_computation.4 | async-start | bytes 5406720
  442.9 11.1 %collective-permute-start = (bf16[2048,1280]{0,1:T(8,128)(2,1)}, bf16[2048,1280]{0,1:T(8,128)(2,1)}, u32[]{:S(2)}, u32[]{:S(2)}) collective-permute-start(bf16[2048,1280]{0,1:T(8,128)(2,1)} %dynamic-slice_bitcast_fusion), channel_id=1, source_target_pairs={{0,32},{32,0},{64,96},{96,64},{128,160},{160,128},{192,224},{224,1... | collective-permute-start | bytes 15728648 | tf_op jit(solution)/shard_map/ppermute | solution.py:156
  690.5 6.0 collective-permute-start.1
  696.6 9.4 %collective-permute-start.2 = (bf16[64,1280]{0,1:T(8,128)(2,1)S(1)}, bf16[64,1280]{0,1:T(8,128)(2,1)S(1)}, u32[]{:S(2)}, u32[]{:S(2)}) collective-permute-start(bf16[64,1280]{0,1:T(8,128)(2,1)S(1)} %add_convert_fusion.1), channel_id=1, source_target_pairs={{0,128},{32,160},{64,192},{96,224},{128,0},{160,32},{192,64},{224,... | collective-permute-start | bytes 491528 | tf_op jit(solution)/shard_map/ppermute | solution.py:162
  706.1 17.5 %copy-start.8 = (bf16[32,128,64]{1,2,0:T(8,128)(2,1)S(1)}, bf16[32,128,64]{1,2,0:T(8,128)(2,1)}, u32[]{:S(2)}) copy-start(bf16[32,128,64]{1,2,0:T(8,128)(2,1)} %get-tuple-element.164) | copy-start | bytes 1572868
  706.2 18.5 %collective-permute-start.3 = (bf16[64,1280]{0,1:T(8,128)(2,1)S(1)}, bf16[64,1280]{0,1:T(8,128)(2,1)S(1)}, u32[]{:S(2)}, u32[]{:S(2)}) collective-permute-start(bf16[64,1280]{0,1:T(8,128)(2,1)S(1)} %add_convert_fusion), channel_id=1, source_target_pairs={{0,32},{32,0},{64,96},{96,64},{128,160},{160,128},{192,224},{224,1... | collective-permute-start | bytes 491528 | tf_op jit(solution)/shard_map/ppermute | solution.py:165
  (47 other events, 178.1 us)
Sparse Core Ops, SparseCore 0:
  11.2 111.6 all-gather.1
  471.5 217.8 reduce-scatter.3
